TPU v7x, 32 devices: a whole 2x2x4 slice. The times are simulated.
32 devices in a mesh: member: 2 (over y), vocab: 16 (over z, x, core).
Axes of the slice: x: 2, y: 2, z: 4, core: 2. Of those that a mesh axis runs over, the one named last changes fastest.
Arguments:
- hidden: bfloat16 [2, 512, 2048], P('member', None, 'vocab'), as said below
- norm_gain: bfloat16 [2, 2048], P('member', 'vocab'), may hold values from 0.5 to 1.5
- head: bfloat16 [2, 2048, 64128], P('member', None, 'vocab'), as said below
- pool_weight: float32 [2], P('member'), may hold values from 0.25 to 1
Outputs:
- log_probs: float32 [512, 64128], P('member', 'vocab')
- agreement: float32 [512], P('member')
Inputs may be any that keep to these rules, and one draw needn't show every extreme that they name: `hidden`: finite values; every member's row has a root mean square over its 2048 features between 0.1 and 100. `head`: finite values, each at most 60 in magnitude, so that a row's logits may reach about a thousand in magnitude.
All inputs are finite; a program needn't handle non-finite values.
Results may differ from a plain program's by a relative error of at most 0.00052.
Values may be sent and summed in bfloat16 or wider, within the bound.
No kernel may reach another device: no remote copies, remote signals or barrier semaphores. Data moves between devices by JAX's collectives and lax.ppermute only.
A program may use at most 128 MiB of HBM per device.

v0:
```python
import jax
import jax.numpy as jnp
from jax import lax
from jax.sharding import PartitionSpec as P

epsilon = 1e-05


def softmax_offset(values, first_pass):
    local_peak = jnp.max(values, axis=1)
    if first_pass:
        row_peak = lax.pmax(local_peak, "vocab")
        summed = lax.psum(jnp.sum(jnp.exp(values - row_peak[:, None]), axis=1), "vocab")
    else:
        row_peak = lax.pmax(local_peak, "vocab")
        summed = lax.psum(jnp.sum(jnp.exp(values - row_peak[:, None]), axis=1), "vocab")
    return row_peak + jnp.log(summed)


def on_device(hidden, norm_gain, head, pool_weight):
    states = hidden[0]
    weights = head[0]
    row_count = states.shape[0]
    narrowed = states.astype(jnp.float32)
    squares = lax.psum(jnp.sum(narrowed * narrowed, axis=1), "vocab")
    width_all = narrowed.shape[1] * lax.axis_size("vocab")
    scaling = lax.rsqrt(squares / width_all + epsilon)[:, None]
    normed = (narrowed * scaling * norm_gain.astype(jnp.float32)).astype(jnp.bfloat16)
    logits = jnp.dot(
        lax.all_gather(normed, "vocab", axis=1, tiled=True),
        weights,
        preferred_element_type=jnp.float32,
    )
    member_lse = softmax_offset(logits, True)
    weighted = pool_weight[0] * (logits - member_lse[:, None])
    share = row_count // lax.axis_size("member")
    pooled_all = lax.psum(weighted, "member")
    kept_rows = lax.dynamic_slice_in_dim(pooled_all, lax.axis_index("member") * share, share, 0)
    agreement = softmax_offset(kept_rows, False)
    return (kept_rows - agreement[:, None], agreement)


def solution(mesh):
    in_specs = (
        P("member", None, "vocab"),
        P("member", "vocab"),
        P("member", None, "vocab"),
        P("member"),
    )
    out_specs = (P("member", "vocab"), P("member"))
    return jax.shard_map(
        on_device, mesh=mesh, in_specs=in_specs, out_specs=out_specs, check_vma=False
    )
```

profile of v0, /device:TPU:0, one launch (start us, length us, event | category | flops | bytes accessed | tf_op | source)
XLA Modules:
  0.0 442.6 jit_solution(5408095204166017930)
XLA Ops:
  7.2 0.0 all-gather.2.cloned.1.call-start
  7.2 1.1 fusion.2
  8.3 34.9 %psum.28 = f32[512]{0:T(512)S(1)} all-reduce(f32[512]{0:T(512)S(1)} %fusion.2), channel_id=1, replica_groups=mesh['member'=2,'vocab'=16] {'vocab'}, use_global_device_ids=true, to_apply=%region_1.0 | all-reduce | flops 512 | bytes 4096 | tf_op jit(solution)/shard_map/psum | solution.py:25
  43.2 0.7 bitcast_convert_fusion
  43.8 1.7 fusion.4
  45.5 0.0 all-gather.2.cloned.1.call-update
  45.6 0.0 all-reduce.2.cloned.1.call-start
  46.3 37.9 %all-gather.2.cloned.1.call-done = bf16[512,2048]{1,0:T(8,128)(2,1)} async-done(((bf16[512,128]{1,0:T(8,128)(2,1)}), bf16[512,2048]{1,0:T(8,128)(2,1)}) %all-gather.2.cloned.1.call-update) | async-done | bytes 2097168 | tf_op jit(solution)/shard_map/all_gather | solution.py:30
  84.2 14.4 %fusion.5 = (f32[512]{0:T(512)S(1)}, f32[512,4008]{0,1:T(8,128)}) fusion(bf16[512,2048]{1,0:T(8,128)(2,1)} %all-gather.2.cloned.1.call-done, bf16[1,2048,4008]{1,2,0:T(8,128)(2,1)} %param.6), kind=kOutput, calls=%fused_computation.16 | convolution fusion | flops 8407436800 | bytes 26724352 | tf_op jit(solution)/shard_map/dot_general | solution.py:29
  98.6 31.6 %pmax.14 = f32[512]{0:T(512)S(1)} all-reduce(f32[512]{0:T(512)S(1)} %get-tuple-element.2), channel_id=1, replica_groups=mesh['member'=2,'vocab'=16] {'vocab'}, use_global_device_ids=true, to_apply=%region_3.0 | all-reduce | flops 512 | bytes 4096 | tf_op jit(solution)/shard_map/pmax | solution.py:12
  130.1 4.5 %exponential_reduce_fusion = f32[512]{0:T(512)S(1)} fusion(f32[512,4008]{0,1:T(8,128)} %get-tuple-element.3, f32[512]{0:T(512)S(1)} %pmax.14), kind=kLoop, calls=%fused_computation.3 | loop fusion | flops 4103680 | bytes 8212480 | tf_op jit(solution)/shard_map/reduce_sum | solution.py:13
  134.6 29.5 %psum.29 = f32[512]{0:T(512)S(1)} all-reduce(f32[512]{0:T(512)S(1)} %exponential_reduce_fusion), channel_id=1, replica_groups=mesh['member'=2,'vocab'=16] {'vocab'}, use_global_device_ids=true, to_apply=%region_5.0 | all-reduce | flops 512 | bytes 4096 | tf_op jit(solution)/shard_map/psum | solution.py:13
  164.1 7.6 %subtract_multiply_fusion = f32[512,4008]{0,1:T(8,128)} fusion(f32[512,4008]{0,1:T(8,128)} %get-tuple-element.3, f32[512]{0:T(512)S(1)} %log_add_fusion, f32[]{:T(128)} %bitcast.14), kind=kLoop, calls=%fused_computation.2 | loop fusion | flops 4104192 | bytes 16418820 | tf_op jit(solution)/shard_map/mul | solution.py:35
  171.7 0.0 all-reduce.2.cloned.1.call-update
  171.7 191.5 %all-reduce.2.cloned.1.call-done = f32[512,4008]{0,1:T(8,128)} async-done(((f32[512,4008]{0,1:T(8,128)}), f32[512,4008]{0,1:T(8,128)}) %all-reduce.2.cloned.1.call-update) | async-done | bytes 8208400 | tf_op jit(solution)/shard_map/psum | solution.py:37
  363.2 2.7 dynamic-slice_reduce_fusion
  365.9 33.1 %pmax.15 = f32[256]{0:T(256)S(1)} all-reduce(f32[256]{0:T(256)S(1)} %dynamic-slice_reduce_fusion), channel_id=1, replica_groups=mesh['member'=2,'vocab'=16] {'vocab'}, use_global_device_ids=true, to_apply=%region_8.0 | all-reduce | flops 256 | bytes 2048 | tf_op jit(solution)/shard_map/pmax | solution.py:15
  399.1 2.8 exponential_reduce_fusion.1
  401.9 29.5 %psum.31 = f32[256]{0:T(256)S(1)} all-reduce(f32[256]{0:T(256)S(1)} %exponential_reduce_fusion.1), channel_id=1, replica_groups=mesh['member'=2,'vocab'=16] {'vocab'}, use_global_device_ids=true, to_apply=%region_10.0 | all-reduce | flops 256 | bytes 2048 | tf_op jit(solution)/shard_map/psum | solution.py:16
  431.4 0.0 copy-start
  431.4 4.4 dynamic-slice_subtract_fusion
  435.8 0.0 copy-done
  (3 shorter events, 0.0 us)
Async XLA Ops:
  7.2 77.0 %all-gather.2.cloned.1.call-start = ((), (), s32[]{:S(2)}) async-start(), calls=%async_computation | async-start | bytes 2228224 | tf_op jit(solution)/shard_map/all_gather | solution.py:30
  45.6 317.7 %all-reduce.2.cloned.1.call-start = ((), (), s32[]{:S(2)}) async-start(), calls=%async_computation.1 | async-start | bytes 16416768 | tf_op jit(solution)/shard_map/psum | solution.py:37
  431.4 4.4 copy-start
Sparse Core Ops, SparseCore 0:
  45.7 38.4 all-gather.1
  171.8 191.3 all-reduce.1
where the time goes:
time: 443 us
  waiting for transfers between devices  229 us (52%)
  blocking collectives  159 us (36%)
  other arithmetic  25.4 us (6%)
  between operations  14.7 us (3%)
  matrix products  14.4 us (3%)
    psum x1, waiting for transfers between devices, on_device(): pooled_all = lax.psum(weighted, 'member')  192 us
    pmax x2, blocking collectives, softmax_offset(): row_peak = lax.pmax(local_peak, 'vocab')  64.7 us
    psum x2, blocking collectives, softmax_offset(): lax.psum(jnp.sum(jnp.exp(values - row_peak[:, None]), axis=1), 'vocab')  59 us
    all_gather x1, waiting for transfers between devices, on_device(): lax.all_gather(normed, 'vocab', axis=1, tiled=True)  37.9 us
    psum x1, blocking collectives, on_device(): squares = lax.psum(jnp.sum(narrowed * narrowed, axis=1), 'vocab')  34.9 us
    dot_general x1, matrix products, on_device(): jnp.dot(lax.all_gather(normed, 'vocab', axis=1, tiled=True), weights, pre...  14.4 us
  transfers between devices with their start and end apart: 2, of which 2 were waited for; matrix products, arithmetic and copies ran while one was open for 0% of the time, Pallas kernels for 0%

commit v1 on v0

--- a/solution.py
+++ b/solution.py
@@ -4,6 +4,27 @@
 from jax.sharding import PartitionSpec as P
 
 epsilon = 1e-05
+
+
+def laid_out(blocks, dim):
+    blocks = jnp.moveaxis(blocks, 0, dim)
+    shape = blocks.shape
+    return blocks.reshape(*shape[:dim], shape[dim] * shape[dim + 1], *shape[dim + 2 :])
+
+
+def collected_by_bits(value, axis):
+    size, index = (lax.axis_size(axis), lax.axis_index(axis))
+    pieces, bit = (value[None], 1)
+    while bit < size:
+        theirs = lax.ppermute(pieces, axis, [(i, i ^ bit) for i in range(size)])
+        low = index & bit == 0
+        pieces = jnp.concatenate([jnp.where(low, pieces, theirs), jnp.where(low, theirs, pieces)])
+        bit *= 2
+    return pieces
+
+
+def doubled_up(x, axis, dim):
+    return laid_out(collected_by_bits(x, axis), dim)
 
 
 def softmax_offset(values, first_pass):
@@ -26,11 +47,7 @@
     width_all = narrowed.shape[1] * lax.axis_size("vocab")
     scaling = lax.rsqrt(squares / width_all + epsilon)[:, None]
     normed = (narrowed * scaling * norm_gain.astype(jnp.float32)).astype(jnp.bfloat16)
-    logits = jnp.dot(
-        lax.all_gather(normed, "vocab", axis=1, tiled=True),
-        weights,
-        preferred_element_type=jnp.float32,
-    )
+    logits = jnp.dot(doubled_up(normed, "vocab", 1), weights, preferred_element_type=jnp.float32)
     member_lse = softmax_offset(logits, True)
     weighted = pool_weight[0] * (logits - member_lse[:, None])
     share = row_count // lax.axis_size("member")

time: 443 us -> 471 us (1.063)
  waiting for transfers between devices: 229 us -> 261 us
    ppermute x0 -> x4, waiting for transfers between devices: none -> 69 us  [collected_by_bits(): theirs = lax.ppermute(pieces, axis, [(i, i ^ bit) for i in range(size)])]
    all_gather x1 -> x0, waiting for transfers between devices: 37.9 us -> none  [on_device(): lax.all_gather(normed, 'vocab', axis=1, tiled=True)]
  transfers between devices with their start and end apart: 2 -> 5, of which waited for: 2 -> 5; matrix products, arithmetic and copies ran while one was open for 0% -> 0% of each run, Pallas kernels for 0% -> 0%
where the time goes in v1:
time: 471 us
  waiting for transfers between devices  261 us (55%)
  blocking collectives  156 us (33%)
  other arithmetic  23.5 us (5%)
  between operations  14.8 us (3%)
  matrix products  14.1 us (3%)
    psum x1, waiting for transfers between devices, on_device(): pooled_all = lax.psum(weighted, 'member')  192 us
    ppermute x4, waiting for transfers between devices, collected_by_bits(): theirs = lax.ppermute(pieces, axis, [(i, i ^ bit) for i in range(size)])  69 us
    pmax x2, blocking collectives, softmax_offset(): row_peak = lax.pmax(local_peak, 'vocab')  62.6 us
    psum x2, blocking collectives, softmax_offset(): lax.psum(jnp.sum(jnp.exp(values - row_peak[:, None]), axis=1), 'vocab')  59 us
    psum x1, blocking collectives, on_device(): squares = lax.psum(jnp.sum(narrowed * narrowed, axis=1), 'vocab')  34.9 us
    dot_general x1, matrix products, on_device(): jnp.dot(doubled_up(normed, 'vocab', 1), weights, preferred_element_type=j...  14.1 us
  transfers between devices with their start and end apart: 5, of which 5 were waited for; matrix products, arithmetic and copies ran while one was open for 0% of the time, Pallas kernels for 0%

profile of v1, /device:TPU:0, one launch (start us, length us, event | category | flops | bytes accessed | tf_op | source)
XLA Modules:
  0.0 470.8 jit_solution(7198621762765088229)
XLA Ops:
  7.2 0.0 all-reduce.2.cloned.1.call-start
  7.2 0.7 bitcast_convert_fusion
  7.9 1.0 copy.6
  8.9 34.9 %psum.28 = f32[512]{0:T(512)S(1)} all-reduce(f32[512]{0:T(512)S(1)} %fusion.2), channel_id=1, replica_groups=mesh['member'=2,'vocab'=16] {'vocab'}, use_global_device_ids=true, to_apply=%region_1.0 | all-reduce | flops 512 | bytes 4096 | tf_op jit(solution)/shard_map/psum | solution.py:46
  43.8 0.1 fusion.4
  43.9 0.1 collective-permute-start
  44.0 1.3 collective-permute-done
  45.3 0.1 broadcast_select_fusion.7
  45.5 0.1 collective-permute-start.1
  45.6 8.3 %collective-permute-done.1 = bf16[2,512,128]{1,2,0:T(8,128)(2,1)S(1)} collective-permute-done((bf16[2,512,128]{1,2,0:T(8,128)(2,1)S(1)}, bf16[2,512,128]{1,2,0:T(8,128)(2,1)S(1)}, u32[]{:S(2)}, u32[]{:S(2)}) %collective-permute-start.1) | collective-permute-done | bytes 262176 | tf_op jit(solution)/shard_map/ppermute | solution.py:19
  54.0 0.1 collective-permute-start.2
  54.1 13.1 %collective-permute-done.2 = bf16[4,512,128]{1,2,0:T(8,128)(2,1)S(1)} collective-permute-done((bf16[4,512,128]{1,2,0:T(8,128)(2,1)S(1)}, bf16[4,512,128]{1,2,0:T(8,128)(2,1)S(1)}, u32[]{:S(2)}, u32[]{:S(2)}) %collective-permute-start.2) | collective-permute-done | bytes 524320 | tf_op jit(solution)/shard_map/ppermute | solution.py:19
  67.2 0.1 broadcast_select_fusion.3
  67.3 0.1 pad_maximum_fusion.1
  67.4 0.1 collective-permute-start.3
  68.2 46.2 %collective-permute-done.3 = bf16[8,512,128]{1,2,0:T(8,128)(2,1)S(1)} collective-permute-done((bf16[8,512,128]{1,2,0:T(8,128)(2,1)S(1)}, bf16[8,512,128]{1,2,0:T(8,128)(2,1)S(1)}, u32[]{:S(2)}, u32[]{:S(2)}) %collective-permute-start.3) | collective-permute-done | bytes 1048608 | tf_op jit(solution)/shard_map/ppermute | solution.py:19
  114.3 0.1 broadcast_select_fusion.1
  114.5 0.2 pad_maximum_fusion
  114.7 14.1 %fusion.5 = (f32[512]{0:T(512)S(1)}, f32[512,4008]{0,1:T(8,128)}) fusion(bf16[512,2048]{0,1:T(8,128)(2,1)S(1)} %bitcast.14, bf16[1,2048,4008]{1,2,0:T(8,128)(2,1)} %param.6), kind=kOutput, calls=%fused_computation.28 | convolution fusion | flops 8407436800 | bytes 26724352 | tf_op jit(solution)/shard_map/dot_general | solution.py:50
  128.8 29.5 %pmax.14 = f32[512]{0:T(512)S(1)} all-reduce(f32[512]{0:T(512)S(1)} %get-tuple-element.10), channel_id=1, replica_groups=mesh['member'=2,'vocab'=16] {'vocab'}, use_global_device_ids=true, to_apply=%region_3.4 | all-reduce | flops 512 | bytes 4096 | tf_op jit(solution)/shard_map/pmax | solution.py:33
  158.3 4.5 exponential_reduce_fusion
  162.7 29.5 %psum.29 = f32[512]{0:T(512)S(1)} all-reduce(f32[512]{0:T(512)S(1)} %exponential_reduce_fusion), channel_id=1, replica_groups=mesh['member'=2,'vocab'=16] {'vocab'}, use_global_device_ids=true, to_apply=%region_5.6 | all-reduce | flops 512 | bytes 4096 | tf_op jit(solution)/shard_map/psum | solution.py:34
  192.2 7.6 %subtract_multiply_fusion = f32[512,4008]{0,1:T(8,128)} fusion(f32[512,4008]{0,1:T(8,128)} %get-tuple-element.11, f32[512]{0:T(512)S(1)} %log_add_fusion, f32[]{:T(128)} %bitcast.13), kind=kLoop, calls=%fused_computation.2 | loop fusion | flops 4104192 | bytes 16418820 | tf_op jit(solution)/shard_map/mul | solution.py:52
  199.8 0.0 all-reduce.2.cloned.1.call-update
  199.8 191.6 %all-reduce.2.cloned.1.call-done = f32[512,4008]{0,1:T(8,128)} async-done(((f32[512,4008]{0,1:T(8,128)}), f32[512,4008]{0,1:T(8,128)}) %all-reduce.2.cloned.1.call-update) | async-done | bytes 8208400 | tf_op jit(solution)/shard_map/psum | solution.py:54
  391.4 2.7 dynamic-slice_reduce_fusion
  394.1 33.1 %pmax.15 = f32[256]{0:T(256)S(1)} all-reduce(f32[256]{0:T(256)S(1)} %dynamic-slice_reduce_fusion), channel_id=1, replica_groups=mesh['member'=2,'vocab'=16] {'vocab'}, use_global_device_ids=true, to_apply=%region_8.9 | all-reduce | flops 256 | bytes 2048 | tf_op jit(solution)/shard_map/pmax | solution.py:36
  427.2 2.8 exponential_reduce_fusion.1
  430.0 29.5 %psum.31 = f32[256]{0:T(256)S(1)} all-reduce(f32[256]{0:T(256)S(1)} %exponential_reduce_fusion.1), channel_id=1, replica_groups=mesh['member'=2,'vocab'=16] {'vocab'}, use_global_device_ids=true, to_apply=%region_10.11 | all-reduce | flops 256 | bytes 2048 | tf_op jit(solution)/shard_map/psum | solution.py:37
  459.5 0.0 copy-start
  459.5 4.4 dynamic-slice_subtract_fusion
  463.9 0.0 copy-done
  (7 shorter events, 0.2 us)
Async XLA Ops:
  7.2 384.2 %all-reduce.2.cloned.1.call-start = ((), (), s32[]{:S(2)}) async-start(), calls=%async_computation | async-start | bytes 16416768 | tf_op jit(solution)/shard_map/psum | solution.py:54
  43.9 1.4 collective-permute-start
  45.5 8.4 %collective-permute-start.1 = (bf16[2,512,128]{1,2,0:T(8,128)(2,1)S(1)}, bf16[2,512,128]{1,2,0:T(8,128)(2,1)S(1)}, u32[]{:S(2)}, u32[]{:S(2)}) collective-permute-start(bf16[2,512,128]{1,2,0:T(8,128)(2,1)S(1)} %pad_maximum_fusion.3), channel_id=1, source_target_pairs={{0,2},{1,3},{2,0},{3,1},{4,6},{5,7},{6,4},{7,5},{8,10},{9,11},{10,... | collective-permute-start | bytes 786440 | tf_op jit(solution)/shard_map/ppermute | solution.py:19
  54.0 13.2 %collective-permute-start.2 = (bf16[4,512,128]{1,2,0:T(8,128)(2,1)S(1)}, bf16[4,512,128]{1,2,0:T(8,128)(2,1)S(1)}, u32[]{:S(2)}, u32[]{:S(2)}) collective-permute-start(bf16[4,512,128]{1,2,0:T(8,128)(2,1)S(1)} %pad_maximum_fusion.2), channel_id=1, source_target_pairs={{0,4},{1,5},{2,6},{3,7},{4,0},{5,1},{6,2},{7,3},{8,12},{9,13},{10,... | collective-permute-start | bytes 1572872 | tf_op jit(solution)/shard_map/ppermute | solution.py:19
  67.4 46.9 %collective-permute-start.3 = (bf16[8,512,128]{1,2,0:T(8,128)(2,1)S(1)}, bf16[8,512,128]{1,2,0:T(8,128)(2,1)S(1)}, u32[]{:S(2)}, u32[]{:S(2)}) collective-permute-start(bf16[8,512,128]{1,2,0:T(8,128)(2,1)S(1)} %pad_maximum_fusion.1), channel_id=1, source_target_pairs={{0,8},{1,9},{2,10},{3,11},{4,12},{5,13},{6,14},{7,15},{8,0},{9,1},... | collective-permute-start | bytes 3145736 | tf_op jit(solution)/shard_map/ppermute | solution.py:19
  459.5 4.4 copy-start
Sparse Core Ops, SparseCore 0:
  199.9 191.3 all-reduce.1
